TPU v7x, 256 devices: a whole 4x4x8 slice. The times are simulated.
256 devices in a mesh: seq: 16 (over x, y), grp: 16 (over z, core).
Axes of the slice: x: 4, y: 4, z: 8, core: 2. Of those that a mesh axis runs over, the one named last changes fastest.
Arguments:
- query_rows: bfloat16 [16, 2048, 4096], P('grp', 'seq'), may hold values from -6 to 6
- key_rows: bfloat16 [16, 2048, 1024], P('grp', 'seq'), may hold values from -6 to 6
- value_rows: bfloat16 [16, 2048, 1024], P('grp', 'seq'), may hold values from -27 to 27
- doc_of_block: int32 [16, 16], P('grp'), may hold values from 0 to 3, never falling along the last dimension, each value on 1 to 8 neighbouring positions
- expert_ids: int32 [16, 2048, 2], P('grp', 'seq'), may hold values from 0 to 7, as said below
- gate_weights: float32 [16, 2048, 2], P('grp', 'seq'), may hold values from 0.1 to 0.9
- norm_gain: float32 [4096], replicated, may hold values from 0.1 to 1.9
- w_in: bfloat16 [2, 7168, 4096], P(None, ('seq', 'grp')), may hold values from -0.09375 to 0.09375
- w_down: bfloat16 [7168, 4096], P(('seq', 'grp')), may hold values from -0.0625 to 0.0625
Outputs:
- layer_out: bfloat16 [16, 2048, 4096], P('grp', 'seq')
Inputs may be any that keep to these rules, and one draw needn't show every extreme that they name: `expert_ids`: each token names 2 different experts; in each aligned block of 128 tokens along a sequence (the tokens of one device) at most 40 tokens name expert 0, and in every draw some block has exactly 40 such tokens.
All inputs are finite; a program needn't handle non-finite values.
Results may differ from a plain program's by a relative error of at most 0.014.
Values may be sent and summed in bfloat16 or wider, within the bound.
No kernel may reach another device: no remote copies, remote signals or barrier semaphores. Data moves between devices by JAX's collectives and lax.ppermute only.
A program may use at most 128 MiB of HBM per device.

v0:
```python
import math
import jax
import jax.numpy as jnp
from jax import lax
from jax.sharding import PartitionSpec as P

QH = 32
KVH = 8
HD = 128
BLK = 128
CAP = 40
EPS = 1e-05
NEG = -1e30


def project_in(gathered, piece):
    return jnp.einsum("rd,khd->krh", gathered, piece, preferred_element_type=jnp.float32)


def activate(gate_up):
    return (jax.nn.silu(gate_up[0]) * gate_up[1]).astype(jnp.bfloat16)


def add_down(hidden, piece):
    return jnp.dot(hidden, piece, preferred_element_type=jnp.float32)


def attend(query_all, key_all, value_all, token_doc, per_dev, kv_local):
    seq_length = query_all.shape[1]
    tile_rows = min(512, seq_length)
    tile_count = seq_length // tile_rows
    per_kv = per_dev // kv_local
    inv_root = 1.0 / math.sqrt(HD)
    query_split = query_all[0].reshape(seq_length, kv_local, per_kv, HD)
    key_split = key_all[0].reshape(seq_length, kv_local, HD)
    value_split = value_all[0].reshape(seq_length, kv_local, HD)
    outputs = []
    for q_index in range(tile_count):
        query_tile = query_split[q_index * tile_rows : (q_index + 1) * tile_rows]
        doc_query = token_doc[q_index * tile_rows : (q_index + 1) * tile_rows]
        allowed_row = doc_query[:, None] == token_doc[None, :]
        scores = (
            jnp.einsum("qkgd,tkd->kgqt", query_tile, key_split, preferred_element_type=jnp.float32)
            * inv_root
        )
        scores = jnp.where(allowed_row, scores, NEG)
        highest = jnp.max(scores, axis=3, keepdims=True)
        weights = jnp.exp(scores - highest)
        denom = jnp.sum(weights, axis=3, keepdims=True)
        mixed = jnp.einsum(
            "kgqt,tkd->qkgd",
            weights.astype(jnp.bfloat16),
            value_split,
            preferred_element_type=jnp.float32,
        )
        mixed = mixed / jnp.transpose(denom, (2, 0, 1, 3))
        outputs.append(mixed.reshape(tile_rows, per_dev * HD).astype(jnp.bfloat16))
    return jnp.concatenate(outputs, axis=0)[None]


def shards(
    query_rows,
    key_rows,
    value_rows,
    doc_of_block,
    expert_ids,
    gate_weights,
    norm_gain,
    w_in,
    w_down,
):
    seq_count = lax.axis_size("seq")
    tok_count = query_rows.shape[1]
    per_dev = QH // seq_count
    repeat_count = max(1, 4 // per_dev)
    kv_local = KVH * repeat_count // seq_count
    key_send = jnp.repeat(key_rows.reshape(1, tok_count, KVH, HD), repeat_count, axis=2).reshape(
        1, tok_count, KVH * repeat_count * HD
    )
    value_send = jnp.repeat(
        value_rows.reshape(1, tok_count, KVH, HD), repeat_count, axis=2
    ).reshape(1, tok_count, KVH * repeat_count * HD)
    query_all, key_all, value_all = (
        lax.all_to_all(query_rows, "seq", split_axis=2, concat_axis=1, tiled=True),
        lax.all_to_all(key_send, "seq", split_axis=2, concat_axis=1, tiled=True),
        lax.all_to_all(value_send, "seq", split_axis=2, concat_axis=1, tiled=True),
    )
    token_doc = jnp.repeat(doc_of_block[0], BLK)
    attended = attend(query_all, key_all, value_all, token_doc, per_dev, kv_local)
    attn_tokens = lax.all_to_all(attended, "seq", split_axis=1, concat_axis=2, tiled=True)
    attn_float = attn_tokens[0].astype(jnp.float32)
    spread = jnp.mean(attn_float * attn_float, axis=-1, keepdims=True)
    normed = (attn_float * lax.rsqrt(spread + EPS) * norm_gain).astype(jnp.bfloat16)
    chosen = expert_ids[0] == 0
    routed = jnp.any(chosen, axis=-1)
    gate_share = jnp.sum(jnp.where(chosen, gate_weights[0], 0.0), axis=-1)
    slot_index = jnp.cumsum(routed.astype(jnp.int32)) - 1
    onehot = (slot_index[None, :] == jnp.arange(CAP, dtype=jnp.int32)[:, None]) & routed[None, :]
    dispatched = jnp.dot(
        onehot.astype(jnp.bfloat16), normed, preferred_element_type=jnp.float32
    ).astype(jnp.bfloat16)
    gathered = lax.all_gather(dispatched, "grp", axis=0, tiled=True)
    gate_up = project_in(gathered, lax.all_gather(w_in, "seq", axis=1, tiled=True))
    hidden = activate(gate_up)
    terms = add_down(hidden, lax.all_gather(w_down, "seq", axis=0, tiled=True))
    returned = lax.psum_scatter(
        terms.astype(jnp.bfloat16), "grp", scatter_dimension=0, tiled=True
    ).astype(jnp.float32)
    picked_rows = jnp.take(returned, jnp.clip(slot_index, 0, CAP - 1), axis=0)
    expert_out = jnp.where(routed[:, None], picked_rows, 0.0)
    layer_out = attn_float + gate_share[:, None] * expert_out
    return layer_out.astype(jnp.bfloat16)[None]


def solution(mesh):
    return jax.shard_map(
        shards,
        mesh=mesh,
        in_specs=(
            P("grp", "seq", None),
            P("grp", "seq", None),
            P("grp", "seq", None),
            P("grp", None),
            P("grp", "seq", None),
            P("grp", "seq", None),
            P(),
            P(None, ("seq", "grp"), None),
            P(("seq", "grp"), None),
        ),
        out_specs=P("grp", "seq", None),
        check_vma=False,
    )
```

profile of v0, /device:TPU:2, one launch (start us, length us, event | category | flops | bytes accessed | tf_op | source)
XLA Modules:
  0.0 441.8 jit_solution(3743156761703894871)
XLA Ops:
  6.5 1.2 copy.112
  7.9 8.1 %copy.145 = bf16[1,128,2048]{1,0,2:T(2,128)(2,1)S(1)} copy(bf16[1,128,2048]{1,2,0:T(8,128)(2,1)S(1)} %bitcast.306) | data formatting | bytes 1048576 | tf_op jit(solution)/shard_map/broadcast_in_dim | solution.py:77
  16.5 11.5 %reduce.20 = bf16[2048,128]{1,0:T(8,128)(2,1)S(1)} reduce(bf16[2048,1,128]{2,1,0:T(2,128)(2,1)S(1)} %bitcast.304, bf16[]{:T(256)} %broadcast.226), dimensions={1}, to_apply=%bitcast.292.reduce_sub_computation | reduce | bytes 1048578
  29.0 7.5 %all-to-all-start = ((bf16[16,2,8192]{2,1,0:T(2,128)(2,1)}), bf16[16,2,8192]{2,1,0:T(2,128)(2,1)S(1)}, u32[]{:S(2)}, u32[]{:S(2)}) async-start(bf16[16,2,8192]{2,1,0:T(2,128)(2,1)} %reshape.333), calls=%async_computation | async-start | bytes 1048576 | tf_op jit(solution)/shard_map/all_to_all | solution.py:85
  36.5 10.8 %all-gather.9.cloned.1.call-start = ((), (), s32[]{:S(2)}) async-start(), calls=%async_computation.8 | async-start | bytes 4456448 | tf_op jit(solution)/shard_map/all_gather | solution.py:105
  47.3 1.1 copy.113
  48.5 8.1 %copy.144 = bf16[1,128,2048]{1,0,2:T(2,128)(2,1)S(1)} copy(bf16[1,128,2048]{1,2,0:T(8,128)(2,1)S(1)} %bitcast.307) | data formatting | bytes 1048576 | tf_op jit(solution)/shard_map/broadcast_in_dim | solution.py:80
  56.6 11.5 %reduce.19 = bf16[2048,128]{1,0:T(8,128)(2,1)S(1)} reduce(bf16[2048,1,128]{2,1,0:T(2,128)(2,1)S(1)} %bitcast.305, bf16[]{:T(256)} %broadcast.226), dimensions={1}, to_apply=%bitcast.291.reduce_sub_computation | reduce | bytes 1048578
  69.1 7.2 %all-to-all-start.2 = ((bf16[16,2,8192]{2,1,0:T(2,128)(2,1)}), bf16[16,2,8192]{2,1,0:T(2,128)(2,1)}, u32[]{:S(2)}, u32[]{:S(2)}) async-start(bf16[16,2,8192]{2,1,0:T(2,128)(2,1)} %reshape.331), calls=%async_computation.2 | async-start | bytes 1048576 | tf_op jit(solution)/shard_map/all_to_all | solution.py:86
  76.4 2.8 copy.84
  79.2 22.4 %reduce.21 = bf16[4096,128]{1,0:T(8,128)(2,1)S(1)} reduce(bf16[4096,1,128]{2,1,0:T(2,128)(2,1)S(1)} %bitcast.299, bf16[]{:T(256)} %broadcast.226), dimensions={1}, to_apply=%bitcast.272.reduce_sub_computation | reduce | bytes 2097154
  101.6 1.1 reshape.335
  102.9 7.7 %all-to-all-start.1 = ((bf16[16,2,16384]{2,1,0:T(2,128)(2,1)}), bf16[16,2,16384]{2,1,0:T(2,128)(2,1)S(1)}, u32[]{:S(2)}, u32[]{:S(2)}) async-start(bf16[16,2,16384]{2,1,0:T(2,128)(2,1)} %reshape.335), calls=%async_computation.1 | async-start | bytes 2097152 | tf_op jit(solution)/shard_map/all_to_all | solution.py:84
  110.7 3.8 broadcast_compare_fusion.3
  114.5 2.2 reshape.334
  117.8 2.2 reshape.332
  121.5 3.1 all-to-all-done.1
  126.1 3.3 fusion.10
  129.4 2.0 fusion
  131.5 2.6 fusion.59
  134.4 2.9 fusion.11
  137.4 2.2 fusion.2
  139.6 2.6 fusion.65
  142.6 2.9 fusion.12
  145.5 2.0 fusion.4
  147.6 3.3 fusion.71
  152.2 2.2 fusion.13
  154.4 2.2 fusion.6
  156.7 2.6 fusion.77
  159.5 11.7 %copy.143 = bf16[1,2048,256]{2,0,1:T(2,128)(2,1)S(1)} copy(bf16[1,2048,256]{2,1,0:T(8,128)(2,1)S(1)} %maximum_bitcast_fusion) | data formatting | bytes 2097152 | tf_op jit(solution)/shard_map/broadcast_in_dim | solution.py:58
  171.3 10.6 %reduce.22 = bf16[2048,256]{1,0:T(8,128)(2,1)S(1)} reduce(bf16[2048,1,256]{2,1,0:T(2,128)(2,1)S(1)} %bitcast.297, bf16[]{:T(256)} %broadcast.226), dimensions={1}, to_apply=%bitcast.290.reduce_sub_computation | reduce | bytes 2097154
  181.9 1.1 reshape.337
  183.0 5.6 %all-to-all-start.3 = ((bf16[16,2,16384]{2,1,0:T(2,128)(2,1)}), bf16[16,2,16384]{2,1,0:T(2,128)(2,1)S(1)}, u32[]{:S(2)}, u32[]{:S(2)}) async-start(bf16[16,2,16384]{2,1,0:T(2,128)(2,1)} %reshape.337), calls=%async_computation.3 | async-start | bytes 2097152 | tf_op jit(solution)/shard_map/all_to_all | solution.py:90
  189.1 13.6 %all-to-all-done.3 = bf16[16,2,16384]{2,1,0:T(2,128)(2,1)S(1)} async-done(((bf16[16,2,16384]{2,1,0:T(2,128)(2,1)}), bf16[16,2,16384]{2,1,0:T(2,128)(2,1)S(1)}, u32[]{:S(2)}, u32[]{:S(2)}) %all-to-all-start.3) | async-done | bytes 1048608 | tf_op jit(solution)/shard_map/all_to_all | solution.py:90
  203.7 1.2 copy.105
  205.0 1.6 copy.117
  206.6 15.4 %multiply_reduce_fusion = f32[2048]{0:T(1024)S(1)} fusion(bf16[2048,1,256]{2,1,0:T(2,128)(2,1)S(1)} %reshape.338), kind=kLoop, calls=%fused_computation.44 | loop fusion | flops 1570816 | bytes 1056768 | tf_op jit(solution)/shard_map/reduce_sum | solution.py:92
  222.1 1.1 convolution_convert_fusion.1
  224.0 5.1 %reshape.324 = bf16[448,4096]{1,0:T(8,128)(2,1)} reshape(bf16[16,28,4096]{2,1,0:T(8,128)(2,1)} %all-gather.9.cloned.1.call-done) | data formatting | bytes 7340032
  229.1 38.4 %all-gather.5.cloned.1.call-done = bf16[640,4096]{1,0:T(8,128)(2,1)} async-done(((bf16[40,4096]{1,0:T(8,128)(2,1)}), bf16[640,4096]{1,0:T(8,128)(2,1)}) %all-gather.5.cloned.1.call-update) | async-done | bytes 5242896 | tf_op jit(solution)/shard_map/all_gather | solution.py:102
  267.5 72.1 %all-gather.7.cloned.1.call-done = bf16[2,448,4096]{2,0,1:T(2,128)(2,1)} async-done(((bf16[2,28,4096]{2,0,1:T(2,128)(2,1)}), bf16[2,448,4096]{2,0,1:T(2,128)(2,1)}) %all-gather.7.cloned.1.call-update) | async-done | bytes 7340048 | tf_op jit(solution)/shard_map/all_gather | solution.py:103
  339.6 18.5 %fusion.35 = f32[2,640,448]{1,2,0:T(8,128)S(1)} fusion(bf16[2,448,4096]{2,0,1:T(2,128)(2,1)} %all-gather.7.cloned.1.call-done, bf16[640,4096]{1,0:T(8,128)(2,1)} %all-gather.5.cloned.1.call-done), kind=kOutput, calls=%fused_computation.49 | convolution fusion | flops 4697620480 | bytes 14876672 | tf_op jit(solution)/shard_map/rd,khd->krh/dot_general | solution.py:17
  358.2 4.8 %convolution_convert_fusion = bf16[640,4096]{1,0:T(8,128)(2,1)} fusion(bf16[448,4096]{1,0:T(8,128)(2,1)S(1)} %copy-done.4, f32[2,640,448]{1,2,0:T(8,128)S(1)} %fusion.35), kind=kOutput, calls=%fused_computation.23 | convolution fusion | flops 2353152000 | bytes 11206656 | tf_op jit(solution)/shard_map/dot_general | solution.py:25
  363.0 2.6 copy.142
  365.6 1.7 reshape.310
  367.4 60.8 %reduce-scatter.2.cloned.1.call-done = bf16[40,4096]{1,0:T(8,128)(2,1)} async-done(((bf16[640,4096]{1,0:T(8,128)(2,1)}), bf16[40,4096]{1,0:T(8,128)(2,1)}) %reduce-scatter.2.cloned.1.call-update) | async-done | bytes 327696 | tf_op jit(solution)/shard_map/reduce_scatter | solution.py:106
  429.2 2.6 gather_fusion
  431.7 3.1 fusion.34
  (84 shorter events, 12.5 us)
Async XLA Ops:
  6.5 69.8 %copy-start.13 = (s32[1,16]{1,0:T(1,128)S(1)}, s32[1,16]{1,0:T(1,128)}, u32[]{:S(2)}) copy-start(s32[1,16]{1,0:T(1,128)} %param.12) | copy-start | bytes 196
  6.5 69.9 %copy-start.6 = (bf16[1,128,4096]{2,1,0:T(8,128)(2,1)S(1)}, bf16[1,128,4096]{2,1,0:T(8,128)(2,1)}, u32[]{:S(2)}) copy-start(bf16[1,128,4096]{2,1,0:T(8,128)(2,1)} %param.9) | copy-start | bytes 3145732
  29.0 40.1 %all-to-all-start = ((bf16[16,2,8192]{2,1,0:T(2,128)(2,1)}), bf16[16,2,8192]{2,1,0:T(2,128)(2,1)S(1)}, u32[]{:S(2)}, u32[]{:S(2)}) async-start(bf16[16,2,8192]{2,1,0:T(2,128)(2,1)} %reshape.333), calls=%async_computation | async-start | bytes 1048576 | tf_op jit(solution)/shard_map/all_to_all | solution.py:85
  36.5 187.5 %all-gather.9.cloned.1.call-start = ((), (), s32[]{:S(2)}) async-start(), calls=%async_computation.8 | async-start | bytes 4456448 | tf_op jit(solution)/shard_map/all_gather | solution.py:105
  69.1 7.2 %copy-start.5 = (bf16[16,2,8192]{2,1,0:T(2,128)(2,1)}, bf16[16,2,8192]{2,1,0:T(2,128)(2,1)S(1)}, u32[]{:S(2)}) copy-start(bf16[16,2,8192]{2,1,0:T(2,128)(2,1)S(1)} %all-to-all-done) | copy-start | bytes 1572868
  69.1 33.8 %all-to-all-start.2 = ((bf16[16,2,8192]{2,1,0:T(2,128)(2,1)}), bf16[16,2,8192]{2,1,0:T(2,128)(2,1)}, u32[]{:S(2)}, u32[]{:S(2)}) async-start(bf16[16,2,8192]{2,1,0:T(2,128)(2,1)} %reshape.331), calls=%async_computation.2 | async-start | bytes 1048576 | tf_op jit(solution)/shard_map/all_to_all | solution.py:86
  102.9 21.7 %all-to-all-start.1 = ((bf16[16,2,16384]{2,1,0:T(2,128)(2,1)}), bf16[16,2,16384]{2,1,0:T(2,128)(2,1)S(1)}, u32[]{:S(2)}, u32[]{:S(2)}) async-start(bf16[16,2,16384]{2,1,0:T(2,128)(2,1)} %reshape.335), calls=%async_computation.1 | async-start | bytes 2097152 | tf_op jit(solution)/shard_map/all_to_all | solution.py:84
  125.8 3.6 copy-start.3
  126.1 5.3 %copy-start.8 = (bf16[2048,128,1]{0,1,2:T(8,128)(2,1)S(1)}, bf16[2048,128,1]{0,1,2:T(8,128)(2,1)}, u32[]{:S(2)}) copy-start(bf16[2048,128,1]{0,1,2:T(8,128)(2,1)} %reshape.326) | copy-start | bytes 1572868
  131.4 3.0 copy-start.2
  134.4 5.1 %copy-start.9 = (bf16[2048,128,1]{0,1,2:T(8,128)(2,1)S(1)}, bf16[2048,128,1]{0,1,2:T(8,128)(2,1)}, u32[]{:S(2)}) copy-start(bf16[2048,128,1]{0,1,2:T(8,128)(2,1)} %reshape.326) | copy-start | bytes 1572868
  139.6 3.0 copy-start.1
  142.6 5.0 %copy-start.10 = (bf16[2048,128,1]{0,1,2:T(8,128)(2,1)S(1)}, bf16[2048,128,1]{0,1,2:T(8,128)(2,1)}, u32[]{:S(2)}) copy-start(bf16[2048,128,1]{0,1,2:T(8,128)(2,1)} %reshape.326) | copy-start | bytes 1572868
  147.5 4.6 %copy-start = (pred[512,2048]{0,1:T(8,128)(4,1)S(1)}, pred[512,2048]{0,1:T(8,128)(4,1)}, u32[]{:S(2)}) copy-start(pred[512,2048]{0,1:T(8,128)(4,1)} %get-tuple-element.14) | copy-start | bytes 3145732
  147.6 4.6 %copy-start.7 = (bf16[1,16,128,128]{3,2,1,0:T(8,128)(2,1)S(1)}, bf16[1,16,128,128]{3,2,1,0:T(8,128)(2,1)}, u32[]{:S(2)}) copy-start(bf16[1,16,128,128]{3,2,1,0:T(8,128)(2,1)} %copy.83) | copy-start | bytes 1572868
  152.2 4.5 %copy-start.11 = (bf16[2048,128,1]{0,1,2:T(8,128)(2,1)S(1)}, bf16[2048,128,1]{0,1,2:T(8,128)(2,1)}, u32[]{:S(2)}) copy-start(bf16[2048,128,1]{0,1,2:T(8,128)(2,1)} %reshape.326) | copy-start | bytes 1572868
  159.3 29.3 %copy-start.14 = (s32[1,128,2]{1,2,0:T(2,128)S(1)}, s32[1,128,2]{1,2,0:T(2,128)}, u32[]{:S(2)}) copy-start(s32[1,128,2]{1,2,0:T(2,128)} %param.13) | copy-start | bytes 3076
  183.0 39.1 %copy-start.12 = (f32[4096]{0:T(1024)S(1)}, f32[4096]{0:T(1024)}, u32[]{:S(2)}) copy-start(f32[4096]{0:T(1024)} %param.15) | copy-start | bytes 49156
  183.0 19.7 %all-to-all-start.3 = ((bf16[16,2,16384]{2,1,0:T(2,128)(2,1)}), bf16[16,2,16384]{2,1,0:T(2,128)(2,1)S(1)}, u32[]{:S(2)}, u32[]{:S(2)}) async-start(bf16[16,2,16384]{2,1,0:T(2,128)(2,1)} %reshape.337), calls=%async_computation.3 | async-start | bytes 2097152 | tf_op jit(solution)/shard_map/all_to_all | solution.py:90
  188.6 78.9 %all-gather.5.cloned.1.call-start = ((), (), s32[]{:S(2)}) async-start(), calls=%async_computation.5 | async-start | bytes 5570560 | tf_op jit(solution)/shard_map/all_gather | solution.py:102
  223.2 116.4 %all-gather.7.cloned.1.call-start = ((), (), s32[]{:S(2)}) async-start(), calls=%async_computation.6 | async-start | bytes 7798784 | tf_op jit(solution)/shard_map/all_gather | solution.py:103
  223.9 204.2 %reduce-scatter.2.cloned.1.call-start = ((), (), s32[]{:S(2)}) async-start(), calls=%async_computation.7 | async-start | bytes 5570560 | tf_op jit(solution)/shard_map/reduce_scatter | solution.py:106
  339.6 18.6 %copy-start.4 = (bf16[448,4096]{1,0:T(8,128)(2,1)S(1)}, bf16[448,4096]{1,0:T(8,128)(2,1)}, u32[]{:S(2)}) copy-start(bf16[448,4096]{1,0:T(8,128)(2,1)} %reshape.324) | copy-start | bytes 11010052
  358.2 4.8 %copy-start.15 = (f32[1,128,2]{1,2,0:T(2,128)S(1)}, f32[1,128,2]{1,2,0:T(2,128)}, u32[]{:S(2)}) copy-start(f32[1,128,2]{1,2,0:T(2,128)} %param.14) | copy-start | bytes 3076
Sparse Core Ops, SparseCore 0:
  47.4 59.1 all-gather.8
  223.3 44.1 all-gather.4
  270.0 69.6 all-gather.6
  363.1 64.9 reduce-scatter.1
where the time goes:
time: 450 us; the launch traced here: 442 us
  waiting for transfers between devices  189 us (42%)
  other arithmetic  88.2 us (20%)
  local copies, waits for them, and re-layouts  64.8 us (14%)
  matrix products  46.9 us (10%)
  starting transfers between devices  38.9 us (9%)
  between operations  14.1 us (3%)
    all_gather x1, waiting for transfers between devices, shards(): lax.all_gather(w_in, 'seq', axis=1, tiled=True)  72.1 us
    reduce_scatter x1, waiting for transfers between devices, shards(): lax.psum_scatter(terms.astype(jnp.bfloat16), 'grp', scatter_dimension=0,...  60.8 us
    unnamed x4, other arithmetic  56 us
    all_gather x1, waiting for transfers between devices, shards(): gathered = lax.all_gather(dispatched, 'grp', axis=0, tiled=True)  38.4 us
    unnamed x47, local copies, waits for them, and re-layouts  21 us
    dot_general x1, matrix products, project_in(): jnp.einsum('rd,khd->krh', gathered, piece, preferred_element_type=jnp.flo...  18.5 us
    reduce_sum x2, other arithmetic, shards(): spread = jnp.mean(attn_float * attn_float, axis=-1, keepdims=True)  15.4 us
    all_to_all x1, waiting for transfers between devices, shards(): lax.all_to_all(attended, 'seq', split_axis=1, concat_axis=2, tiled=True)  13.6 us
  transfers between devices with their start and end apart: 8, of which 5 were waited for; matrix products, arithmetic and copies ran while one was open for 33% of the time, Pallas kernels for 0%

commit v1 on v0

--- a/solution.py
+++ b/solution.py
@@ -87,7 +87,10 @@
     )
     token_doc = jnp.repeat(doc_of_block[0], BLK)
     attended = attend(query_all, key_all, value_all, token_doc, per_dev, kv_local)
-    attn_tokens = lax.all_to_all(attended, "seq", split_axis=1, concat_axis=2, tiled=True)
+    attn_tokens = jnp.concatenate(
+        lax.all_to_all(jnp.stack(jnp.split(attended, lax.axis_size("seq"), axis=1)), "seq", 0, 0),
+        axis=2,
+    )
     attn_float = attn_tokens[0].astype(jnp.float32)
     spread = jnp.mean(attn_float * attn_float, axis=-1, keepdims=True)
     normed = (attn_float * lax.rsqrt(spread + EPS) * norm_gain).astype(jnp.bfloat16)

time: 450 us -> 405 us (0.900)
  other arithmetic: 88.2 us -> 65 us
  starting transfers between devices: 38.9 us -> 28.2 us
  local copies, waits for them, and re-layouts: 64.8 us -> 54.6 us
    reduce_sum x2 -> x1, other arithmetic: 15.4 us -> 0.56 us  [shards(): spread = jnp.mean(attn_float * attn_float, axis=-1, keepdims=True)]
    broadcast_in_dim x1 -> x0, local copies, waits for them, and re-layouts: 11.7 us -> none  [attend(): return jnp.concatenate(outputs, axis=0)[None]]
    all_gather x1, starting transfers between devices: 10.8 us -> 0.21 us  [shards(): terms = add_down(hidden, lax.all_gather(w_down, 'seq', axis=0, tiled=True))]
    unnamed x4 -> x3, other arithmetic: 56 us -> 45.6 us
    unnamed x47 -> x59, local copies, waits for them, and re-layouts: 21 us -> 26.9 us
  transfers between devices with their start and end apart: 8 -> 8, of which waited for: 5 -> 5; matrix products, arithmetic and copies ran while one was open for 33% -> 28% of each run, Pallas kernels for 0% -> 0%
where the time goes in v1:
time: 405 us; the launch traced here: 397 us
  waiting for transfers between devices  190 us (47%)
  other arithmetic  65 us (16%)
  local copies, waits for them, and re-layouts  54.6 us (13%)
  matrix products  45.6 us (11%)
  starting transfers between devices  28.2 us (7%)
  between operations  13.9 us (3%)
    all_gather x1, waiting for transfers between devices, shards(): lax.all_gather(w_in, 'seq', axis=1, tiled=True)  72.1 us
    reduce_scatter x1, waiting for transfers between devices, shards(): lax.psum_scatter(terms.astype(jnp.bfloat16), 'grp', scatter_dimension=0,...  61.5 us
    unnamed x3, other arithmetic  45.6 us
    all_gather x1, waiting for transfers between devices, shards(): gathered = lax.all_gather(dispatched, 'grp', axis=0, tiled=True)  38.5 us
    unnamed x59, local copies, waits for them, and re-layouts  26.9 us
    dot_general x1, matrix products, project_in(): jnp.einsum('rd,khd->krh', gathered, piece, preferred_element_type=jnp.flo...  18.6 us
    all_to_all x1, waiting for transfers between devices, shards(): lax.all_to_all(jnp.stack(jnp.split(attended, lax.axis_size('seq'), axis=1...  13.6 us
    dot_general x4, matrix products, attend(): jnp.einsum('kgqt,tkd->qkgd', weights.astype(jnp.bfloat16), value_split, p...  11.1 us
  transfers between devices with their start and end apart: 8, of which 5 were waited for; matrix products, arithmetic and copies ran while one was open for 28% of the time, Pallas kernels for 0%

profile of v1, /device:TPU:2, one launch (start us, length us, event | category | flops | bytes accessed | tf_op | source)
XLA Modules:
  0.0 397.3 jit_solution(17470519598905034944)
XLA Ops:
  6.5 1.2 copy.76
  7.9 8.1 %copy.105 = bf16[1,128,2048]{1,0,2:T(2,128)(2,1)S(1)} copy(bf16[1,128,2048]{1,2,0:T(8,128)(2,1)S(1)} %bitcast.359) | data formatting | bytes 1048576 | tf_op jit(solution)/shard_map/broadcast_in_dim | solution.py:77
  16.6 11.6 %reduce.17 = bf16[2048,128]{1,0:T(8,128)(2,1)S(1)} reduce(bf16[2048,1,128]{2,1,0:T(2,128)(2,1)S(1)} %bitcast.357, bf16[]{:T(256)} %broadcast.226), dimensions={1}, to_apply=%bitcast.350.reduce_sub_computation | reduce | bytes 1048578
  28.2 0.9 reshape.323
  29.1 7.5 %all-to-all-start = ((bf16[16,2,8192]{2,1,0:T(2,128)(2,1)}), bf16[16,2,8192]{2,1,0:T(2,128)(2,1)S(1)}, u32[]{:S(2)}, u32[]{:S(2)}) async-start(bf16[16,2,8192]{2,1,0:T(2,128)(2,1)} %reshape.323), calls=%async_computation | async-start | bytes 1048576 | tf_op jit(solution)/shard_map/all_to_all | solution.py:85
  37.3 1.1 copy.77
  38.5 8.1 %copy.104 = bf16[1,128,2048]{1,0,2:T(2,128)(2,1)S(1)} copy(bf16[1,128,2048]{1,2,0:T(8,128)(2,1)S(1)} %bitcast.360) | data formatting | bytes 1048576 | tf_op jit(solution)/shard_map/broadcast_in_dim | solution.py:80
  46.7 11.6 %reduce.16 = bf16[2048,128]{1,0:T(8,128)(2,1)S(1)} reduce(bf16[2048,1,128]{2,1,0:T(2,128)(2,1)S(1)} %bitcast.358, bf16[]{:T(256)} %broadcast.226), dimensions={1}, to_apply=%bitcast.349.reduce_sub_computation | reduce | bytes 1048578
  58.3 0.9 reshape.321
  59.2 7.2 %all-to-all-start.2 = ((bf16[16,2,8192]{2,1,0:T(2,128)(2,1)}), bf16[16,2,8192]{2,1,0:T(2,128)(2,1)}, u32[]{:S(2)}, u32[]{:S(2)}) async-start(bf16[16,2,8192]{2,1,0:T(2,128)(2,1)} %reshape.321), calls=%async_computation.2 | async-start | bytes 1048576 | tf_op jit(solution)/shard_map/all_to_all | solution.py:86
  66.5 2.8 copy.53
  69.3 22.4 %reduce.18 = bf16[4096,128]{1,0:T(8,128)(2,1)S(1)} reduce(bf16[4096,1,128]{2,1,0:T(2,128)(2,1)S(1)} %bitcast.352, bf16[]{:T(256)} %broadcast.226), dimensions={1}, to_apply=%bitcast.335.reduce_sub_computation | reduce | bytes 2097154
  91.7 1.1 reshape.325
  93.0 7.7 %all-to-all-start.1 = ((bf16[16,2,16384]{2,1,0:T(2,128)(2,1)}), bf16[16,2,16384]{2,1,0:T(2,128)(2,1)S(1)}, u32[]{:S(2)}, u32[]{:S(2)}) async-start(bf16[16,2,16384]{2,1,0:T(2,128)(2,1)} %reshape.325), calls=%async_computation.1 | async-start | bytes 2097152 | tf_op jit(solution)/shard_map/all_to_all | solution.py:84
  100.8 3.8 broadcast_compare_fusion.3
  104.6 2.2 reshape.324
  106.9 1.0 copy.52
  108.0 2.2 reshape.322
  110.6 1.0 reshape.316
  111.6 3.1 all-to-all-done.1
  114.7 1.0 reshape.326
  116.5 3.3 fusion.10
  119.8 2.0 fusion
  121.8 2.6 fusion.59
  124.5 2.2 fusion.11
  126.7 2.2 fusion.2
  128.9 3.3 fusion.65
  132.4 2.2 fusion.12
  134.7 2.0 fusion.4
  136.7 2.6 fusion.71
  139.5 2.2 fusion.13
  141.8 2.0 fusion.6
  143.8 2.6 fusion.77
  156.9 5.5 %all-to-all-start.3 = ((bf16[16,1,128,256]{2,3,1,0:T(8,128)(2,1)}), bf16[16,1,128,256]{2,3,1,0:T(8,128)(2,1)S(1)}, u32[]{:S(2)}, u32[]{:S(2)}) async-start(bf16[16,1,128,256]{2,3,1,0:T(8,128)(2,1)} %fusion.91), calls=%async_computation.3 | async-start | bytes 2097152 | tf_op jit(solution)/shard_map/all_to_all | solution.py:91
  162.9 13.6 %all-to-all-done.3 = bf16[16,1,128,256]{2,3,1,0:T(8,128)(2,1)S(1)} async-done(((bf16[16,1,128,256]{2,3,1,0:T(8,128)(2,1)}), bf16[16,1,128,256]{2,3,1,0:T(8,128)(2,1)S(1)}, u32[]{:S(2)}, u32[]{:S(2)}) %all-to-all-start.3) | async-done | bytes 1048608 | tf_op jit(solution)/shard_map/all_to_all | solution.py:91
  177.1 0.7 fusion.32
  177.8 1.2 convolution_convert_fusion.1
  179.8 5.0 %reshape.314 = bf16[448,4096]{1,0:T(8,128)(2,1)} reshape(bf16[16,28,4096]{2,1,0:T(8,128)(2,1)} %all-gather.9.cloned.1.call-done) | data formatting | bytes 7340032
  184.8 38.5 %all-gather.5.cloned.1.call-done = bf16[640,4096]{1,0:T(8,128)(2,1)} async-done(((bf16[40,4096]{1,0:T(8,128)(2,1)}), bf16[640,4096]{1,0:T(8,128)(2,1)}) %all-gather.5.cloned.1.call-update) | async-done | bytes 5242896 | tf_op jit(solution)/shard_map/all_gather | solution.py:105
  223.3 72.1 %all-gather.7.cloned.1.call-done = bf16[2,448,4096]{2,0,1:T(2,128)(2,1)} async-done(((bf16[2,28,4096]{2,0,1:T(2,128)(2,1)}), bf16[2,448,4096]{2,0,1:T(2,128)(2,1)}) %all-gather.7.cloned.1.call-update) | async-done | bytes 7340048 | tf_op jit(solution)/shard_map/all_gather | solution.py:106
  295.4 18.6 %fusion.37 = f32[2,640,448]{1,2,0:T(8,128)S(1)} fusion(bf16[2,448,4096]{2,0,1:T(2,128)(2,1)} %all-gather.7.cloned.1.call-done, bf16[640,4096]{1,0:T(8,128)(2,1)} %all-gather.5.cloned.1.call-done), kind=kOutput, calls=%fused_computation.51 | convolution fusion | flops 4697620480 | bytes 14876672 | tf_op jit(solution)/shard_map/rd,khd->krh/dot_general | solution.py:17
  314.0 4.8 %convolution_convert_fusion = bf16[640,4096]{1,0:T(8,128)(2,1)} fusion(bf16[448,4096]{1,0:T(8,128)(2,1)S(1)} %copy-done.4, f32[2,640,448]{1,2,0:T(8,128)S(1)} %fusion.37), kind=kOutput, calls=%fused_computation.23 | convolution fusion | flops 2353152000 | bytes 11206656 | tf_op jit(solution)/shard_map/dot_general | solution.py:25
  318.9 1.6 convert_element_type.130
  320.4 1.9 copy.78
  322.4 61.5 %reduce-scatter.2.cloned.1.call-done = bf16[40,4096]{1,0:T(8,128)(2,1)} async-done(((bf16[640,4096]{1,0:T(8,128)(2,1)}), bf16[40,4096]{1,0:T(8,128)(2,1)}) %reduce-scatter.2.cloned.1.call-update) | async-done | bytes 327696 | tf_op jit(solution)/shard_map/reduce_scatter | solution.py:109
  383.8 1.0 convert_element_type.125
  384.9 2.6 gather_fusion
  387.4 3.1 fusion.36
  (90 shorter events, 15.8 us)
Async XLA Ops:
  6.5 59.9 %copy-start.13 = (s32[1,16]{1,0:T(1,128)S(1)}, s32[1,16]{1,0:T(1,128)}, u32[]{:S(2)}) copy-start(s32[1,16]{1,0:T(1,128)} %param.12) | copy-start | bytes 196
  6.5 60.0 %copy-start.6 = (bf16[1,128,4096]{2,1,0:T(8,128)(2,1)S(1)}, bf16[1,128,4096]{2,1,0:T(8,128)(2,1)}, u32[]{:S(2)}) copy-start(bf16[1,128,4096]{2,1,0:T(8,128)(2,1)} %param.9) | copy-start | bytes 3145732
  29.1 30.1 %all-to-all-start = ((bf16[16,2,8192]{2,1,0:T(2,128)(2,1)}), bf16[16,2,8192]{2,1,0:T(2,128)(2,1)S(1)}, u32[]{:S(2)}, u32[]{:S(2)}) async-start(bf16[16,2,8192]{2,1,0:T(2,128)(2,1)} %reshape.323), calls=%async_computation | async-start | bytes 1048576 | tf_op jit(solution)/shard_map/all_to_all | solution.py:85
  36.6 143.2 %all-gather.9.cloned.1.call-start = ((), (), s32[]{:S(2)}) async-start(), calls=%async_computation.8 | async-start | bytes 4456448 | tf_op jit(solution)/shard_map/all_gather | solution.py:108
  59.2 7.2 %copy-start.5 = (bf16[16,2,8192]{2,1,0:T(2,128)(2,1)}, bf16[16,2,8192]{2,1,0:T(2,128)(2,1)S(1)}, u32[]{:S(2)}) copy-start(bf16[16,2,8192]{2,1,0:T(2,128)(2,1)S(1)} %all-to-all-done) | copy-start | bytes 1572868
  59.2 33.8 %all-to-all-start.2 = ((bf16[16,2,8192]{2,1,0:T(2,128)(2,1)}), bf16[16,2,8192]{2,1,0:T(2,128)(2,1)}, u32[]{:S(2)}, u32[]{:S(2)}) async-start(bf16[16,2,8192]{2,1,0:T(2,128)(2,1)} %reshape.321), calls=%async_computation.2 | async-start | bytes 1048576 | tf_op jit(solution)/shard_map/all_to_all | solution.py:86
  93.0 21.7 %all-to-all-start.1 = ((bf16[16,2,16384]{2,1,0:T(2,128)(2,1)}), bf16[16,2,16384]{2,1,0:T(2,128)(2,1)S(1)}, u32[]{:S(2)}, u32[]{:S(2)}) async-start(bf16[16,2,16384]{2,1,0:T(2,128)(2,1)} %reshape.325), calls=%async_computation.1 | async-start | bytes 2097152 | tf_op jit(solution)/shard_map/all_to_all | solution.py:84
  115.9 3.8 copy-start.3
  116.5 5.3 %copy-start.8 = (bf16[2048,128,1]{0,1,2:T(8,128)(2,1)S(1)}, bf16[2048,128,1]{0,1,2:T(8,128)(2,1)}, u32[]{:S(2)}) copy-start(bf16[2048,128,1]{0,1,2:T(8,128)(2,1)} %reshape.316) | copy-start | bytes 1572868
  121.8 2.6 copy-start.2
  121.8 2.6 copy-start.7
  128.9 3.5 copy-start.1
  132.4 4.2 %copy-start.9 = (bf16[2048,128,1]{0,1,2:T(8,128)(2,1)S(1)}, bf16[2048,128,1]{0,1,2:T(8,128)(2,1)}, u32[]{:S(2)}) copy-start(bf16[2048,128,1]{0,1,2:T(8,128)(2,1)} %reshape.316) | copy-start | bytes 1572868
  136.7 2.9 copy-start
  139.5 4.3 %copy-start.10 = (bf16[2048,128,1]{0,1,2:T(8,128)(2,1)S(1)}, bf16[2048,128,1]{0,1,2:T(8,128)(2,1)}, u32[]{:S(2)}) copy-start(bf16[2048,128,1]{0,1,2:T(8,128)(2,1)} %reshape.316) | copy-start | bytes 1572868
  143.8 2.7 copy-start.11
  143.8 18.7 %copy-start.14 = (s32[1,128,2]{1,2,0:T(2,128)S(1)}, s32[1,128,2]{1,2,0:T(2,128)}, u32[]{:S(2)}) copy-start(s32[1,128,2]{1,2,0:T(2,128)} %param.13) | copy-start | bytes 3076
  143.8 33.3 %copy-start.12 = (f32[4096]{0:T(1024)S(1)}, f32[4096]{0:T(1024)}, u32[]{:S(2)}) copy-start(f32[4096]{0:T(1024)} %param.15) | copy-start | bytes 49156
  156.9 19.6 %all-to-all-start.3 = ((bf16[16,1,128,256]{2,3,1,0:T(8,128)(2,1)}), bf16[16,1,128,256]{2,3,1,0:T(8,128)(2,1)S(1)}, u32[]{:S(2)}, u32[]{:S(2)}) async-start(bf16[16,1,128,256]{2,3,1,0:T(8,128)(2,1)} %fusion.91), calls=%async_computation.3 | async-start | bytes 2097152 | tf_op jit(solution)/shard_map/all_to_all | solution.py:91
  162.4 60.9 %all-gather.5.cloned.1.call-start = ((), (), s32[]{:S(2)}) async-start(), calls=%async_computation.5 | async-start | bytes 5570560 | tf_op jit(solution)/shard_map/all_gather | solution.py:105
  179.0 116.4 %all-gather.7.cloned.1.call-start = ((), (), s32[]{:S(2)}) async-start(), calls=%async_computation.6 | async-start | bytes 7798784 | tf_op jit(solution)/shard_map/all_gather | solution.py:106
  179.7 204.1 %reduce-scatter.2.cloned.1.call-start = ((), (), s32[]{:S(2)}) async-start(), calls=%async_computation.7 | async-start | bytes 5570560 | tf_op jit(solution)/shard_map/reduce_scatter | solution.py:109
  295.4 18.6 %copy-start.4 = (bf16[448,4096]{1,0:T(8,128)(2,1)S(1)}, bf16[448,4096]{1,0:T(8,128)(2,1)}, u32[]{:S(2)}) copy-start(bf16[448,4096]{1,0:T(8,128)(2,1)} %reshape.314) | copy-start | bytes 11010052
  314.0 4.8 %copy-start.15 = (f32[1,128,2]{1,2,0:T(2,128)S(1)}, f32[1,128,2]{1,2,0:T(2,128)}, u32[]{:S(2)}) copy-start(f32[1,128,2]{1,2,0:T(2,128)} %param.14) | copy-start | bytes 3076
Sparse Core Ops, SparseCore 0:
  39.8 59.1 all-gather.8
  179.1 44.1 all-gather.4
  225.8 69.6 all-gather.6
  318.9 64.8 reduce-scatter.1
